TPU v7x, 256 devices: a whole 4x4x8 slice. The times are simulated.
256 devices in a mesh: dp: 16 (over y, x_lo, core), ctx: 8 (over z), tp: 2 (over x_hi).
Axes of the slice: x: 4 (x_hi: 2, x_lo: 2; x = x_hi * 2 + x_lo), y: 4, z: 8, core: 2. Of those that a mesh axis runs over, the one named last changes fastest.
Arguments:
- tokens: bfloat16 [16, 2048, 8192], P('dp', 'ctx', 'tp'), may hold values from -6 to 6
- queries: bfloat16 [16, 2048, 8192], P('dp', 'ctx', 'tp'), may hold values from -180 to 180
- k_weight: bfloat16 [8192, 512], P('dp', 'tp'), may hold values from -0.0625 to 0.0625
- v_weight: bfloat16 [8192, 512], P('dp', 'tp'), may hold values from -0.0625 to 0.0625
- doc_blocks: int32 [16, 16], P('dp', 'ctx'), may hold values from 0 to 3, never falling along the last dimension, each value on 1 to 8 neighbouring positions
Outputs:
- context: bfloat16 [16, 2048, 8192], P('dp', 'ctx', 'tp')
Inputs may be any that keep to these rules, and one draw needn't show every extreme that they name: `doc_blocks`: along each sequence the document numbers never fall; each document covers 1 to 8 whole blocks, one exactly 8.
All inputs are finite; a program needn't handle non-finite values.
Results may differ from a plain program's by a relative error of at most 0.012.
The roundings to bfloat16 on the way count: a program that leaves them out, or rounds other values in their place, can miss the bound.
Values may be sent and summed in bfloat16 or wider, within the bound.
No kernel may reach another device: no remote copies, remote signals or barrier semaphores. Data moves between devices by JAX's collectives and lax.ppermute only.
A program may use at most 192 MiB of HBM per device.

v0:
```python
import math
import jax
import jax.numpy as jnp
from jax import lax
from jax.sharding import PartitionSpec as P

HD = 128
BLOCK = 128
ROPE_BASE = 500000.0
YARN_FACTOR = 16.0
PRETRAIN_CONTEXT = 8192.0
BETA_FAST = 32.0
BETA_SLOW = 1.0
ATTN_FACTOR = (1.0 + 0.1 * math.log(16.0)) ** 2
MASKED_SCORE = -1e30


def yarn_tables(positions):
    counter = jnp.arange(HD // 2, dtype=jnp.float32)
    base_freq = ROPE_BASE ** (-2.0 * counter / HD)
    wave_ratio = PRETRAIN_CONTEXT * base_freq / (2.0 * math.pi)
    ramp_value = jnp.clip((wave_ratio - BETA_SLOW) / (BETA_FAST - BETA_SLOW), 0.0, 1.0)
    frequency = ramp_value * base_freq + (1.0 - ramp_value) * base_freq / YARN_FACTOR
    angles = positions.astype(jnp.float32)[:, None] * frequency[None, :]
    cosine = jnp.cos(angles)
    sine_table = jnp.sin(angles)
    return (
        jnp.concatenate([cosine, cosine], axis=-1),
        jnp.concatenate([sine_table, sine_table], axis=-1),
    )


def rotate(vectors, cosine, sine_table):
    half_width = vectors.shape[-1] // 2
    lower_half = vectors[..., :half_width]
    upper_half = vectors[..., half_width:]
    turned = jnp.concatenate([-upper_half, lower_half], axis=-1)
    return vectors * cosine[:, None, :] + turned * sine_table[:, None, :]


def collect_features(local_tokens):
    return lax.all_gather(local_tokens, "tp", axis=1, tiled=True)


def body(tokens, queries, k_weight, v_weight, doc_blocks):
    local_tokens = tokens[0]
    row_count = local_tokens.shape[0]
    ctx_rank = lax.axis_index("ctx")
    all_docs = lax.all_gather(doc_blocks[0], "ctx", axis=0, tiled=True)
    kv_width = k_weight.shape[1]
    kv_heads = kv_width // HD
    whole = collect_features(local_tokens)
    pieces = (
        lax.all_gather(k_weight, "dp", axis=0, tiled=True),
        lax.all_gather(v_weight, "dp", axis=0, tiled=True),
    )
    height = pieces[0].shape[0]
    key_proj = jnp.dot(whole, pieces[0], preferred_element_type=jnp.float32)
    value_proj = jnp.dot(whole, pieces[1], preferred_element_type=jnp.float32)
    positions = ctx_rank * row_count + jnp.arange(row_count, dtype=jnp.int32)
    cosine, sine_table = yarn_tables(positions)
    key_rows = (
        rotate(key_proj.reshape(row_count, kv_heads, HD), cosine, sine_table)
        .reshape(row_count, kv_width)
        .astype(jnp.bfloat16)
    )
    value_rows = value_proj.astype(jnp.bfloat16)
    local_queries = queries[0]
    query_heads = local_queries.shape[1] // HD
    group_size = query_heads // kv_heads
    query_rot = (
        (
            rotate(
                local_queries.astype(jnp.float32).reshape(row_count, query_heads, HD),
                cosine,
                sine_table,
            )
            * (ATTN_FACTOR / math.sqrt(HD))
        )
        .reshape(row_count, query_heads * HD)
        .astype(jnp.bfloat16)
    )
    token_docs = jnp.repeat(all_docs, BLOCK)
    query_total = query_rot.shape[0]
    query_docs = token_docs[positions]
    grouped = query_rot.reshape(query_total, kv_heads, group_size, HD)
    start_max = jnp.full((kv_heads, group_size, query_total), MASKED_SCORE, jnp.float32)
    start_sum = jnp.zeros((kv_heads, group_size, query_total), jnp.float32)
    start_acc = jnp.zeros((kv_heads, group_size, query_total, HD), jnp.float32)
    key_piece = lax.all_gather(key_rows, "ctx", axis=0, tiled=True)
    value_piece = lax.all_gather(value_rows, "ctx", axis=0, tiled=True)
    height = key_piece.shape[0]
    key_pos = jnp.arange(height, dtype=jnp.int32)
    visible = (key_pos[None, :] <= positions[:, None]) & (
        token_docs[None, :] == query_docs[:, None]
    )

    def update(state):
        running_max, running_sum, running_acc = state
        scores = jnp.einsum(
            "qkgd,nkd->kgqn",
            grouped,
            key_piece.reshape(height, kv_heads, HD),
            preferred_element_type=jnp.float32,
        )
        scores = jnp.where(visible, scores, MASKED_SCORE)
        new_max = jnp.maximum(running_max, jnp.max(scores, axis=-1))
        weights = jnp.where(visible, jnp.exp(scores - new_max[..., None]), 0.0)
        new_sum = jnp.sum(weights, axis=-1)
        new_acc = jnp.einsum(
            "kgqn,nkd->kgqd",
            weights.astype(jnp.bfloat16),
            value_piece.reshape(height, kv_heads, HD),
            preferred_element_type=jnp.float32,
        )
        return (new_max, new_sum, new_acc)

    def unchanged(state):
        return state

    final_max, final_sum, final_acc = lax.cond(
        jnp.any(visible), update, unchanged, (start_max, start_sum, start_acc)
    )
    attended = final_acc / final_sum[..., None]
    context = (
        attended.transpose(2, 0, 1, 3).reshape(query_total, query_heads * HD).astype(jnp.bfloat16)
    )
    return context[None]


def solution(mesh):
    placed = (
        P("dp", "ctx", "tp"),
        P("dp", "ctx", "tp"),
        P("dp", "tp"),
        P("dp", "tp"),
        P("dp", "ctx"),
    )
    return jax.shard_map(
        body, mesh=mesh, in_specs=placed, out_specs=P("dp", "ctx", "tp"), check_vma=False
    )
```

profile of v0, /device:TPU:2, one launch (start us, length us, event | category | flops | bytes accessed | tf_op | source)
XLA Modules:
  0.0 327.5 jit_solution(8934308022742542548)
XLA Ops:
  6.5 0.0 all-gather.16.cloned.1.call-start
  6.5 0.7 all-gather.16.cloned.1.call-update
  7.3 0.0 all-gather.8.cloned.1.call-start
  7.3 0.7 all-gather.8.cloned.1.call-update
  8.0 0.0 all-gather.12.cloned.1.call-start
  8.1 0.7 all-gather.12.cloned.1.call-update
  8.7 0.0 all-gather.10.cloned.1.call-start
  8.8 0.3 multiply_cosine_fusion
  9.2 0.0 copy-start.2
  9.2 0.0 copy-start.1
  9.2 65.3 %all-gather.16.cloned.1.call-done = bf16[1,256,8192]{2,1,0:T(8,128)(2,1)} async-done(((bf16[1,256,4096]{2,1,0:T(8,128)(2,1)}), bf16[1,256,8192]{2,1,0:T(8,128)(2,1)}) %all-gather.16.cloned.1.call-update) | async-done | bytes 4194320 | tf_op jit(solution)/shard_map/all_gather | solution.py:42
  74.5 41.7 %all-gather.8.cloned.1.call-done = bf16[8192,256]{1,0:T(8,128)(2,1)} async-done(((bf16[512,256]{1,0:T(8,128)(2,1)}), bf16[8192,256]{1,0:T(8,128)(2,1)}) %all-gather.8.cloned.1.call-update) | async-done | bytes 4194320 | tf_op jit(solution)/shard_map/all_gather | solution.py:54
  116.2 5.2 %fusion.11 = f32[256,256]{0,1:T(8,128)S(1)} fusion(bf16[8192,256]{1,0:T(8,128)(2,1)} %all-gather.8.cloned.1.call-done, bf16[1,256,8192]{2,1,0:T(8,128)(2,1)} %all-gather.16.cloned.1.call-done), kind=kOutput, calls=%fused_computation.15 | convolution fusion | flops 1073741824 | bytes 8650752 | tf_op jit(solution)/shard_map/dot_general | solution.py:58
  121.5 0.7 fusion.18
  122.2 0.0 all-gather.10.cloned.1.call-update
  122.2 0.0 all-gather.14.cloned.1.call-start
  122.3 0.0 copy-done.2
  122.3 0.6 dynamic-slice
  123.5 0.0 copy-done.1
  123.5 0.1 bitcast_dynamic-update-slice_fusion
  123.6 34.4 %all-gather.12.cloned.1.call-done = bf16[8192,256]{1,0:T(8,128)(2,1)} async-done(((bf16[512,256]{1,0:T(8,128)(2,1)}), bf16[8192,256]{1,0:T(8,128)(2,1)}) %all-gather.12.cloned.1.call-update) | async-done | bytes 4194320 | tf_op jit(solution)/shard_map/all_gather | solution.py:55
  157.9 5.4 %fusion.15 = bf16[256,256]{1,0:T(8,128)(2,1)} fusion(bf16[8192,256]{1,0:T(8,128)(2,1)} %all-gather.12.cloned.1.call-done, bf16[1,256,8192]{2,1,0:T(8,128)(2,1)} %all-gather.16.cloned.1.call-done), kind=kOutput, calls=%fused_computation.23 | convolution fusion | flops 1073807360 | bytes 8519680 | tf_op jit(solution)/shard_map/dot_general | solution.py:59
  163.3 0.0 all-gather.14.cloned.1.call-update
  163.3 3.3 %copy.18 = bf16[1,256,4096]{1,2,0:T(8,128)(2,1)S(1)} copy(bf16[1,256,4096]{2,1,0:T(8,128)(2,1)} %param.8) | data formatting | bytes 4194304 | tf_op args[1]
  166.6 2.3 convert_element_type.65
  168.9 14.0 %all-reduce = s32[16]{0:T(128)S(1)} all-reduce(s32[16]{0:T(128)S(1)} %bitcast_dynamic-update-slice_fusion), channel_id=2, replica_groups=mesh['dp'=16,'ctx'=8,'tp'=2] {'ctx'}, use_global_device_ids=true, to_apply=%add | all-reduce | flops 16 | bytes 128
  183.0 0.1 broadcast_bitcast_fusion
  183.0 1.7 gather_fusion
  184.8 1.3 fusion.14
  186.6 2.5 slice_negate_fusion
  189.1 0.0 copy-start
  189.1 0.5 pad_maximum_fusion
  189.6 1.8 copy-done
  191.3 1.1 multiply_convert_fusion
  192.4 6.9 %all-gather.10.cloned.1.call-done = bf16[2048,256]{0,1:T(8,128)(2,1)} async-done(((bf16[256,256]{0,1:T(8,128)(2,1)}), bf16[2048,256]{0,1:T(8,128)(2,1)}) %all-gather.10.cloned.1.call-update) | async-done | bytes 1048592 | tf_op jit(solution)/shard_map/all_gather | solution.py:90
  199.3 39.1 %all-gather.14.cloned.1.call-done = bf16[2048,256]{1,0:T(8,128)(2,1)} async-done(((bf16[256,256]{1,0:T(8,128)(2,1)}), bf16[2048,256]{1,0:T(8,128)(2,1)}) %all-gather.14.cloned.1.call-update) | async-done | bytes 1048592 | tf_op jit(solution)/shard_map/all_gather | solution.py:91
  238.4 76.0 %conditional.1 = (f32[2,16,256]{2,1,0:T(8,128)S(1)}, f32[2,16,256,128]{3,2,1,0:T(8,128)}) conditional(s32[]{:T(128)} %convert_element_type.53, () %tuple.13, (pred[256,2048]{0,1:T(8,128)(4,1)S(1)}, bf16[2048,256]{0,1:T(8,128)(2,1)}, bf16[256,2,16,128]{0,3,2,1:T(8,128)(2,1)S(1)}, bf16[2048,256]{1,0:T(8,128)(2,1)}) %tuple.14), branch_computations={%region_1.2_spmd, %region_2.5_spmd} | conditional | flops 8757698560 | bytes 213581840 | solution.py:121
  238.4 24.4 %fusion = (f32[2,16,256]{2,1,0:T(8,128)S(1)}, f32[2,2048,256,16]{2,1,3,0:T(8,128)}) fusion(pred[256,2048]{0,1:T(8,128)(4,1)S(1)} %get-tuple-element.13, bf16[2048,2,128,1]{0,2,3,1:T(8,128)(2,1)} %bitcast.55, bf16[256,2,16,128]{0,3,2,1:T(8,128)(2,1)S(1)} %get-tuple-element.27), kind=kOutput, calls=%fused_computation.3 | convolution fusion | flops 4328513536 | bytes 70811648 | tf_op jit(solution)/shard_map/cond/branch_1_fun/qkgd,nkd->kgqn/dot_general | solution.py:100
  262.8 1.3 reshape.84
  264.1 28.7 %fusion.3 = f32[2,16,256,128]{3,2,1,0:T(8,128)} fusion(f32[2,2048,256,16]{2,1,3,0:T(8,128)} %get-tuple-element.30, f32[2,16,256]{2,1,0:T(8,128)S(1)} %broadcast_maximum_fusion, pred[256,2048]{0,1:T(8,128)(4,1)S(1)} %get-tuple-element.13, bf16[2048,2,128,1]{2,1,0,3:T(2,128)(2,1)S(1)} %bitcast.54), kind=kOutput, calls=%fused_computation.6 | convolution fusion | flops 4362076160 | bytes 72908800 | tf_op jit(solution)/shard_map/cond/branch_1_fun/kgqn,nkd->kgqd/dot_general | solution.py:110
  292.9 21.6 %fusion.2 = f32[2,16,256]{2,1,0:T(8,128)S(1)} fusion(f32[2,2048,256,16]{2,1,3,0:T(8,128)} %get-tuple-element.30, f32[2,16,256]{2,1,0:T(8,128)S(1)} %broadcast_maximum_fusion, pred[256,2048]{0,1:T(8,128)(4,1)S(1)} %get-tuple-element.13), kind=kLoop, calls=%fused_computation.5 | loop fusion | flops 67100672 | bytes 67698688 | tf_op jit(solution)/shard_map/cond/branch_1_fun/reduce_sum | solution.py:109
  314.5 2.9 fusion.13
  317.3 1.4 copy.21
  318.7 2.3 convert_element_type.64
  (10 shorter events, 0.1 us)
Async XLA Ops:
  6.5 68.0 %all-gather.16.cloned.1.call-start = ((), (), s32[]{:S(2)}) async-start(), calls=%async_computation.4 | async-start | bytes 6291456 | tf_op jit(solution)/shard_map/all_gather | solution.py:42
  7.3 109.0 %all-gather.8.cloned.1.call-start = ((), (), s32[]{:S(2)}) async-start(), calls=%async_computation | async-start | bytes 4456448 | tf_op jit(solution)/shard_map/all_gather | solution.py:54
  8.0 149.9 %all-gather.12.cloned.1.call-start = ((), (), s32[]{:S(2)}) async-start(), calls=%async_computation.2 | async-start | bytes 4456448 | tf_op jit(solution)/shard_map/all_gather | solution.py:55
  8.7 190.6 %all-gather.10.cloned.1.call-start = ((), (), s32[]{:S(2)}) async-start(), calls=%async_computation.1 | async-start | bytes 1179648 | tf_op jit(solution)/shard_map/all_gather | solution.py:90
  9.2 113.1 %copy-start.2 = (u32[256]{0:T(256)S(1)}, u32[256]{0:T(256)}, u32[]{:S(2)}) copy-start(u32[256]{0:T(256)} %constant.56) | copy-start | bytes 3076
  9.2 114.3 %copy-start.1 = (s32[1,2]{1,0:T(1,128)S(1)}, s32[1,2]{1,0:T(1,128)}, u32[]{:S(2)}) copy-start(s32[1,2]{1,0:T(1,128)} %param.11) | copy-start | bytes 28
  122.2 116.2 %all-gather.14.cloned.1.call-start = ((), (), s32[]{:S(2)}) async-start(), calls=%async_computation.3 | async-start | bytes 1179648 | tf_op jit(solution)/shard_map/all_gather | solution.py:91
  189.1 2.2 copy-start
Sparse Core Ops, SparseCore 0:
  9.1 65.3 all-gather.15
  76.4 39.8 all-gather.7
  118.1 39.7 all-gather.11
  159.5 39.7 all-gather.9
  200.9 37.4 all-gather.13
where the time goes:
time: 328 us
  waiting for transfers between devices  190 us (58%)
  matrix products  63.7 us (19%)
  other arithmetic  33.1 us (10%)
  between operations  14.4 us (4%)
  blocking collectives  14 us (4%)
  local copies, waits for them, and re-layouts  12.5 us (4%)
    all_gather x1, waiting for transfers between devices, collect_features(): return lax.all_gather(local_tokens, 'tp', axis=1, tiled=True)  65.3 us
    all_gather x1, waiting for transfers between devices, body(): lax.all_gather(k_weight, 'dp', axis=0, tiled=True)  41.7 us
    all_gather x1, waiting for transfers between devices, body(): value_piece = lax.all_gather(value_rows, 'ctx', axis=0, tiled=True)  39.1 us
    all_gather x1, waiting for transfers between devices, body(): lax.all_gather(v_weight, 'dp', axis=0, tiled=True)  34.4 us
    dot_general x1, matrix products, update(): jnp.einsum('kgqn,nkd->kgqd', weights.astype(jnp.bfloat16), value_piece.re...  28.7 us
    dot_general x1, matrix products, update(): jnp.einsum('qkgd,nkd->kgqn', grouped, key_piece.reshape(height, kv_heads,...  24.4 us
    reduce_sum x1, other arithmetic, update(): new_sum = jnp.sum(weights, axis=-1)  21.6 us
    unnamed x1, blocking collectives  14 us
  transfers between devices with their start and end apart: 5, of which 5 were waited for; matrix products, arithmetic and copies ran while one was open for 8% of the time, Pallas kernels for 0%

commit v1 on v0

--- a/solution.py
+++ b/solution.py
@@ -87,7 +87,15 @@
     start_max = jnp.full((kv_heads, group_size, query_total), MASKED_SCORE, jnp.float32)
     start_sum = jnp.zeros((kv_heads, group_size, query_total), jnp.float32)
     start_acc = jnp.zeros((kv_heads, group_size, query_total, HD), jnp.float32)
-    key_piece = lax.all_gather(key_rows, "ctx", axis=0, tiled=True)
+    key_piece = jnp.concatenate(
+        lax.all_to_all(
+            jnp.stack([key_rows] * lax.axis_size("ctx")),
+            axis_name="ctx",
+            split_axis=0,
+            concat_axis=0,
+        ),
+        axis=0,
+    )
     value_piece = lax.all_gather(value_rows, "ctx", axis=0, tiled=True)
     height = key_piece.shape[0]
     key_pos = jnp.arange(height, dtype=jnp.int32)

time: 328 us -> 294 us (0.90)
  waiting for transfers between devices: 190 us -> 145 us
  starting transfers between devices: 0.16 us -> 7.13 us
  local copies, waits for them, and re-layouts: 12.5 us -> 17.1 us
    all_gather x1, waiting for transfers between devices: 39.1 us -> 9.93 us  [body(): value_piece = lax.all_gather(value_rows, 'ctx', axis=0, tiled=True)]
    all_to_all x0 -> x1, starting transfers between devices: none -> 7.01 us  [body(): lax.all_to_all(jnp.stack([key_rows] * lax.axis_size('ctx')), axis_name='c...]
    all_gather x1 -> x0, waiting for transfers between devices: 6.88 us -> none  [body(): key_piece = lax.all_gather(key_rows, 'ctx', axis=0, tiled=True)]
    all_gather x1, waiting for transfers between devices: 34.4 us -> 28.2 us  [body(): lax.all_gather(v_weight, 'dp', axis=0, tiled=True)]
    unnamed x10 -> x6, local copies, waits for them, and re-layouts: 5.72 us -> 7.02 us
  transfers between devices with their start and end apart: 5 -> 5, of which waited for: 5 -> 4; matrix products, arithmetic and copies ran while one was open for 8% -> 9% of each run, Pallas kernels for 0% -> 0%
where the time goes in v1:
time: 294 us
  waiting for transfers between devices  145 us (49%)
  matrix products  63.8 us (22%)
  other arithmetic  32.6 us (11%)
  local copies, waits for them, and re-layouts  17.1 us (6%)
  between operations  14.5 us (5%)
  blocking collectives  13.9 us (5%)
  starting transfers between devices  7.13 us (2%)
    all_gather x1, waiting for transfers between devices, collect_features(): return lax.all_gather(local_tokens, 'tp', axis=1, tiled=True)  62.7 us
    all_gather x1, waiting for transfers between devices, body(): lax.all_gather(k_weight, 'dp', axis=0, tiled=True)  41.7 us
    dot_general x1, matrix products, update(): jnp.einsum('kgqn,nkd->kgqd', weights.astype(jnp.bfloat16), value_piece.re...  28.7 us
    all_gather x1, waiting for transfers between devices, body(): lax.all_gather(v_weight, 'dp', axis=0, tiled=True)  28.2 us
    dot_general x1, matrix products, update(): jnp.einsum('qkgd,nkd->kgqn', grouped, key_piece.reshape(height, kv_heads,...  24.5 us
    reduce_sum x1, other arithmetic, update(): new_sum = jnp.sum(weights, axis=-1)  21.6 us
    unnamed x1, blocking collectives  13.9 us
    all_gather x1, waiting for transfers between devices, body(): value_piece = lax.all_gather(value_rows, 'ctx', axis=0, tiled=True)  9.93 us
  transfers between devices with their start and end apart: 5, of which 4 were waited for; matrix products, arithmetic and copies ran while one was open for 9% of the time, Pallas kernels for 0%

profile of v1, /device:TPU:2, one launch (start us, length us, event | category | flops | bytes accessed | tf_op | source)
XLA Modules:
  0.0 293.7 jit_solution(6552430667657631299)
XLA Ops:
  6.5 0.0 all-gather.13.cloned.1.call-start
  6.5 0.7 all-gather.13.cloned.1.call-update
  7.3 0.0 all-gather.7.cloned.1.call-start
  7.3 0.7 all-gather.7.cloned.1.call-update
  8.0 0.0 all-gather.9.cloned.1.call-start
  8.1 0.7 all-gather.9.cloned.1.call-update
  8.7 1.3 dynamic-slice
  10.7 0.3 multiply_cosine_fusion
  11.0 0.8 bitcast_dynamic-update-slice_fusion
  11.8 62.7 %all-gather.13.cloned.1.call-done = bf16[1,256,8192]{2,1,0:T(8,128)(2,1)} async-done(((bf16[1,256,4096]{2,1,0:T(8,128)(2,1)}), bf16[1,256,8192]{2,1,0:T(8,128)(2,1)}) %all-gather.13.cloned.1.call-update) | async-done | bytes 4194320 | tf_op jit(solution)/shard_map/all_gather | solution.py:42
  74.5 41.7 %all-gather.7.cloned.1.call-done = bf16[8192,256]{1,0:T(8,128)(2,1)} async-done(((bf16[512,256]{1,0:T(8,128)(2,1)}), bf16[8192,256]{1,0:T(8,128)(2,1)}) %all-gather.7.cloned.1.call-update) | async-done | bytes 4194320 | tf_op jit(solution)/shard_map/all_gather | solution.py:54
  116.2 5.2 %fusion.13 = f32[256,256]{0,1:T(8,128)S(1)} fusion(bf16[8192,256]{1,0:T(8,128)(2,1)} %all-gather.7.cloned.1.call-done, bf16[1,256,8192]{2,1,0:T(8,128)(2,1)} %all-gather.13.cloned.1.call-done), kind=kOutput, calls=%fused_computation.17 | convolution fusion | flops 1073741824 | bytes 8650752 | tf_op jit(solution)/shard_map/dot_general | solution.py:58
  121.6 0.1 copy.18
  121.7 1.0 stack.2
  122.7 7.0 %all-to-all-start = ((bf16[8,256,256]{2,1,0:T(8,128)(2,1)}), bf16[8,256,256]{2,1,0:T(8,128)(2,1)}, u32[]{:S(2)}, u32[]{:S(2)}) async-start(bf16[8,256,256]{2,1,0:T(8,128)(2,1)} %stack.2), calls=%async_computation | async-start | bytes 2097152 | tf_op jit(solution)/shard_map/all_to_all | solution.py:91
  129.7 0.0 all-gather.11.cloned.1.call-start
  129.8 28.2 %all-gather.9.cloned.1.call-done = bf16[8192,256]{1,0:T(8,128)(2,1)} async-done(((bf16[512,256]{1,0:T(8,128)(2,1)}), bf16[8192,256]{1,0:T(8,128)(2,1)}) %all-gather.9.cloned.1.call-update) | async-done | bytes 4194320 | tf_op jit(solution)/shard_map/all_gather | solution.py:55
  157.9 5.4 %fusion.17 = bf16[256,256]{1,0:T(8,128)(2,1)} fusion(bf16[8192,256]{1,0:T(8,128)(2,1)} %all-gather.9.cloned.1.call-done, bf16[1,256,8192]{2,1,0:T(8,128)(2,1)} %all-gather.13.cloned.1.call-done), kind=kOutput, calls=%fused_computation.25 | convolution fusion | flops 1073807360 | bytes 8519680 | tf_op jit(solution)/shard_map/dot_general | solution.py:59
  163.3 0.0 all-gather.11.cloned.1.call-update
  163.4 3.3 %copy.19 = bf16[1,256,4096]{1,2,0:T(8,128)(2,1)S(1)} copy(bf16[1,256,4096]{2,1,0:T(8,128)(2,1)} %param.8) | data formatting | bytes 4194304 | tf_op args[1]
  166.6 2.3 convert_element_type.65
  168.9 13.9 %all-reduce = s32[16]{0:T(128)S(1)} all-reduce(s32[16]{0:T(128)S(1)} %bitcast_dynamic-update-slice_fusion), channel_id=2, replica_groups=mesh['dp'=16,'ctx'=8,'tp'=2] {'ctx'}, use_global_device_ids=true, to_apply=%add | all-reduce | flops 16 | bytes 128
  182.9 0.1 broadcast_bitcast_fusion
  182.9 1.7 gather_fusion
  184.7 1.3 fusion.16
  186.6 2.6 slice_negate_fusion
  189.1 0.0 copy-start
  189.1 0.5 pad_maximum_fusion
  189.6 1.7 copy-done
  191.3 1.1 multiply_convert_fusion
  192.4 0.0 all-to-all-done
  192.4 9.9 %all-gather.11.cloned.1.call-done = bf16[2048,256]{1,0:T(8,128)(2,1)} async-done(((bf16[256,256]{1,0:T(8,128)(2,1)}), bf16[2048,256]{1,0:T(8,128)(2,1)}) %all-gather.11.cloned.1.call-update) | async-done | bytes 1048592 | tf_op jit(solution)/shard_map/all_gather | solution.py:99
  202.3 78.3 %conditional.1 = (f32[2,16,256]{2,1,0:T(8,128)S(1)}, f32[2,16,256,128]{3,2,1,0:T(8,128)}) conditional(s32[]{:T(128)} %convert_element_type.53, () %tuple.13, (pred[256,2048]{0,1:T(8,128)(4,1)S(1)}, bf16[8,256,256]{2,1,0:T(8,128)(2,1)}, bf16[256,2,16,128]{0,3,2,1:T(8,128)(2,1)S(1)}, bf16[2048,256]{1,0:T(8,128)(2,1)}) %tuple.14), branch_computations={%region_1.2_spmd, %region_2.5_spmd} | conditional | flops 8757698560 | bytes 215678992 | solution.py:129
  202.3 2.1 reshape_reshape.2
  204.4 24.5 %fusion = (f32[2,16,256]{2,1,0:T(8,128)S(1)}, f32[2,2048,256,16]{2,1,3,0:T(8,128)}) fusion(pred[256,2048]{0,1:T(8,128)(4,1)S(1)} %get-tuple-element.13, bf16[256,2,16,128]{0,3,2,1:T(8,128)(2,1)S(1)} %get-tuple-element.23, bf16[2048,2,128,1]{2,1,0,3:T(2,128)(2,1)} %bitcast.48), kind=kOutput, calls=%fused_computation.3 | convolution fusion | flops 4328513536 | bytes 70811648 | tf_op jit(solution)/shard_map/cond/branch_1_fun/qkgd,nkd->kgqn/dot_general | solution.py:108
  229.0 1.3 reshape.83
  230.3 28.7 %fusion.3 = f32[2,16,256,128]{3,2,1,0:T(8,128)} fusion(f32[2,2048,256,16]{2,1,3,0:T(8,128)} %get-tuple-element.26, f32[2,16,256]{2,1,0:T(8,128)S(1)} %broadcast_maximum_fusion, pred[256,2048]{0,1:T(8,128)(4,1)S(1)} %get-tuple-element.13, bf16[2048,2,128,1]{2,1,0,3:T(2,128)(2,1)S(1)} %bitcast.50), kind=kOutput, calls=%fused_computation.6 | convolution fusion | flops 4362076160 | bytes 72908800 | tf_op jit(solution)/shard_map/cond/branch_1_fun/kgqn,nkd->kgqd/dot_general | solution.py:118
  259.1 21.6 %fusion.2 = f32[2,16,256]{2,1,0:T(8,128)S(1)} fusion(f32[2,2048,256,16]{2,1,3,0:T(8,128)} %get-tuple-element.26, f32[2,16,256]{2,1,0:T(8,128)S(1)} %broadcast_maximum_fusion, pred[256,2048]{0,1:T(8,128)(4,1)S(1)} %get-tuple-element.13), kind=kLoop, calls=%fused_computation.5 | loop fusion | flops 67100672 | bytes 67698688 | tf_op jit(solution)/shard_map/cond/branch_1_fun/reduce_sum | solution.py:117
  280.7 2.9 fusion.15
  283.5 1.4 copy.21
  284.9 2.3 convert_element_type.64
  (11 shorter events, 0.2 us)
Async XLA Ops:
  6.5 68.0 %all-gather.13.cloned.1.call-start = ((), (), s32[]{:S(2)}) async-start(), calls=%async_computation.4 | async-start | bytes 6291456 | tf_op jit(solution)/shard_map/all_gather | solution.py:42
  7.3 109.0 %all-gather.7.cloned.1.call-start = ((), (), s32[]{:S(2)}) async-start(), calls=%async_computation.1 | async-start | bytes 4456448 | tf_op jit(solution)/shard_map/all_gather | solution.py:54
  8.0 149.9 %all-gather.9.cloned.1.call-start = ((), (), s32[]{:S(2)}) async-start(), calls=%async_computation.2 | async-start | bytes 4456448 | tf_op jit(solution)/shard_map/all_gather | solution.py:55
  122.7 69.7 %all-to-all-start = ((bf16[8,256,256]{2,1,0:T(8,128)(2,1)}), bf16[8,256,256]{2,1,0:T(8,128)(2,1)}, u32[]{:S(2)}, u32[]{:S(2)}) async-start(bf16[8,256,256]{2,1,0:T(8,128)(2,1)} %stack.2), calls=%async_computation | async-start | bytes 2097152 | tf_op jit(solution)/shard_map/all_to_all | solution.py:91
  129.7 72.6 %all-gather.11.cloned.1.call-start = ((), (), s32[]{:S(2)}) async-start(), calls=%async_computation.3 | async-start | bytes 1179648 | tf_op jit(solution)/shard_map/all_gather | solution.py:99
  189.1 2.2 copy-start
Sparse Core Ops, SparseCore 0:
  9.1 65.3 all-gather.12
  76.4 39.8 all-gather.6
  118.1 39.7 all-gather.8
  163.5 38.8 all-gather.10
